TPU v7x, 128 devices: a whole 4x4x4 slice. The times are simulated.
128 devices in a mesh: row: 4 (over z), col: 32 (over x, y, core).
Axes of the slice: x: 4, y: 4, z: 4, core: 2. Of those that a mesh axis runs over, the one named last changes fastest.
Arguments:
- matrix_real: bfloat16 [512, 16384], P('col', 'row'), may hold values from -0.25 to 0.25
- matrix_imag: bfloat16 [512, 16384], P('col', 'row'), may hold values from -0.25 to 0.25
- valence_index: int32 [512], P('col'), may hold values from 0 to 15
- conduction_index: int32 [512], P('col'), may hold values from 0 to 31
- valence_energy: float32 [16], replicated, may hold values from -1.5 to -0.1
- conduction_energy: float32 [32], replicated, may hold values from 0.1 to 2
- frequency: float32 [2], replicated, may hold values from 0.2 to 2
Outputs:
- chi_real: bfloat16 [2, 16384, 16384], P(None, 'row', 'col')
- chi_imag: bfloat16 [2, 16384, 16384], P(None, 'row', 'col')
All inputs are finite; a program needn't handle non-finite values.
Results may differ from a plain program's by a relative error of at most 0.005.
Values may be sent and summed in bfloat16 or wider, within the bound.
No kernel may reach another device: no remote copies, remote signals or barrier semaphores. Data moves between devices by JAX's collectives and lax.ppermute only.
A program may use at most 192 MiB of HBM per device.

v0:
```python
import jax
import jax.numpy as jnp
from jax import lax
from jax.sharding import PartitionSpec as P


def lookup(indices, table):
    count = table.shape[0]
    picks = indices[:, None] == lax.broadcasted_iota(jnp.int32, (1, count), 1)
    return jnp.sum(jnp.where(picks, table[None, :], 0.0), axis=1)


def contract(left_side, right_side):
    return lax.dot_general(
        left_side, right_side, (((0,), (0,)), ((), ())), preferred_element_type=jnp.float32
    )


def on_device(
    matrix_real,
    matrix_imag,
    valence_index,
    conduction_index,
    valence_energy,
    conduction_energy,
    frequency,
):
    all_valence, all_conduction = (
        lax.all_gather(valence_index, "col", axis=0, tiled=True),
        lax.all_gather(conduction_index, "col", axis=0, tiled=True),
    )
    gap = lookup(all_conduction, conduction_energy) - lookup(all_valence, valence_energy)
    spread_real, spread_imag = (
        lax.all_gather(matrix_real, "row", axis=1, tiled=True),
        lax.all_gather(matrix_imag, "row", axis=1, tiled=True),
    )
    column_real, column_imag = (
        lax.all_to_all(spread_real, "col", split_axis=1, concat_axis=0, tiled=True),
        lax.all_to_all(spread_imag, "col", split_axis=1, concat_axis=0, tiled=True),
    )
    width = column_real.shape[1]
    wide_real = column_real.astype(jnp.float32)
    wide_imag = column_imag.astype(jnp.float32)
    upper_parts = []
    lower_parts = []
    for index in range(frequency.shape[0]):
        omega = frequency[index]
        weight = 4.0 * gap / (gap * gap + omega * omega)
        scaled_real = (weight[:, None] * wide_real).astype(jnp.bfloat16)
        scaled_imag = (weight[:, None] * wide_imag).astype(jnp.bfloat16)
        upper_parts.extend([scaled_real, scaled_imag])
        lower_parts.extend([scaled_imag, -scaled_real])
    upper_side = jnp.concatenate(upper_parts, axis=1)
    lower_side = jnp.concatenate(lower_parts, axis=1)
    right_side = jnp.concatenate([upper_side, lower_side], axis=0)
    block_real, block_imag = (
        lax.all_to_all(matrix_real, "col", split_axis=1, concat_axis=0, tiled=True),
        lax.all_to_all(matrix_imag, "col", split_axis=1, concat_axis=0, tiled=True),
    )
    stacked = jnp.concatenate([block_real, block_imag], axis=0)
    joined = contract(lax.all_gather(stacked, "col", axis=1, tiled=True), right_side)
    real_out = []
    imag_out = []
    for index in range(frequency.shape[0]):
        start = 2 * width * index
        real_out.append((-joined[:, start : start + width]).astype(jnp.bfloat16))
        imag_out.append((-joined[:, start + width : start + 2 * width]).astype(jnp.bfloat16))
    return (jnp.stack(real_out, axis=0), jnp.stack(imag_out, axis=0))


def solution(mesh):
    placed = (P("col", "row"), P("col", "row"), P("col"), P("col"), P(), P(), P())
    return jax.shard_map(
        on_device,
        mesh=mesh,
        in_specs=placed,
        out_specs=(P(None, "row", "col"), P(None, "row", "col")),
        check_vma=False,
    )
```

profile of v0, /device:TPU:1, one launch (start us, length us, event | category | flops | bytes accessed | tf_op | source)
XLA Modules:
  0.0 199.1 jit_solution(13468990475961677798)
XLA Ops:
  7.2 1.6 copy_bitcast_fusion.3
  8.7 8.6 %all-to-all-start = ((bf16[16,32,128]{2,0,1:T(8,128)(2,1)}), bf16[16,32,128]{2,0,1:T(8,128)(2,1)S(1)}, u32[]{:S(2)}, u32[]{:S(2)}) async-start(bf16[16,32,128]{2,0,1:T(8,128)(2,1)} %copy_bitcast_fusion.3), calls=%async_computation | async-start | bytes 262144 | tf_op jit(solution)/shard_map/all_to_all | solution.py:57
  17.3 0.0 all-gather.2.cloned.1.call-start
  17.4 0.9 copy_bitcast_fusion.2
  18.3 6.7 %all-to-all-done = bf16[16,32,128]{2,0,1:T(8,128)(2,1)S(1)} async-done(((bf16[16,32,128]{2,0,1:T(8,128)(2,1)}), bf16[16,32,128]{2,0,1:T(8,128)(2,1)S(1)}, u32[]{:S(2)}, u32[]{:S(2)}) %all-to-all-start) | async-done | bytes 131104 | tf_op jit(solution)/shard_map/all_to_all | solution.py:57
  25.0 11.3 %all_to_all.64 = bf16[16,32,128]{2,0,1:T(8,128)(2,1)S(1)} all-to-all(bf16[16,32,128]{2,0,1:T(8,128)(2,1)S(1)} %copy_bitcast_fusion.2), channel_id=1, replica_groups=mesh['row'=4,'col'=32] {'col'}, dimensions={1} | all-to-all | bytes 262144 | tf_op jit(solution)/shard_map/all_to_all | solution.py:58
  36.3 0.7 pad_maximum_fusion.2
  37.0 0.0 all-gather.2.cloned.1.call-update
  37.1 12.7 %all_gather.19 = bf16[16,16384]{1,0:T(8,128)(2,1)S(1)} all-gather(bf16[16,4096]{1,0:T(8,128)(2,1)} %param.8), channel_id=1, replica_groups=mesh['row'=4,'col'=32] {'row'}, dimensions={1}, use_global_device_ids=true | all-gather | bytes 655360 | tf_op jit(solution)/shard_map/all_gather | solution.py:35
  49.7 0.9 copy.29
  50.6 5.5 %all-to-all-start.3 = ((bf16[16,32,512]{2,0,1:T(8,128)(2,1)}), bf16[16,32,512]{2,0,1:T(8,128)(2,1)S(1)}, u32[]{:S(2)}, u32[]{:S(2)}) async-start(bf16[16,32,512]{2,0,1:T(8,128)(2,1)} %bitcast.54), calls=%async_computation.3 | async-start | bytes 1048576 | tf_op jit(solution)/shard_map/all_to_all | solution.py:39
  56.1 12.0 %all_gather.18 = bf16[16,16384]{1,0:T(8,128)(2,1)S(1)} all-gather(bf16[16,4096]{1,0:T(8,128)(2,1)} %param.7), channel_id=1, replica_groups=mesh['row'=4,'col'=32] {'row'}, dimensions={1}, use_global_device_ids=true | all-gather | bytes 655360 | tf_op jit(solution)/shard_map/all_gather | solution.py:34
  68.1 0.9 copy.30
  68.9 1.3 dynamic-slice
  70.8 0.9 dynamic-update-slice
  71.7 0.9 dynamic-update-slice.1
  72.5 15.7 %all-reduce.2 = (s32[512]{0:T(512)S(1)}, s32[512]{0:T(512)S(1)}) all-reduce(s32[512]{0:T(512)S(1)} %dynamic-update-slice, s32[512]{0:T(512)S(1)} %dynamic-update-slice.1), channel_id=1, replica_groups=mesh['row'=4,'col'=32] {'col'}, use_global_device_ids=true, to_apply=%add | all-reduce | flops 1024 | bytes 8192
  88.3 0.7 select_reduce_fusion.1
  89.0 0.7 select_reduce_fusion
  89.8 0.0 all-to-all-done.3
  89.8 6.8 %all-to-all-start.2 = ((bf16[16,32,512]{2,0,1:T(8,128)(2,1)}), bf16[16,32,512]{2,0,1:T(8,128)(2,1)S(1)}, u32[]{:S(2)}, u32[]{:S(2)}) async-start(bf16[16,32,512]{2,0,1:T(8,128)(2,1)} %bitcast.55), calls=%async_computation.2 | async-start | bytes 1048576 | tf_op jit(solution)/shard_map/all_to_all | solution.py:38
  96.6 1.3 fusion.33
  100.5 0.2 fusion.24
  100.7 7.6 %all-to-all-done.2 = bf16[16,32,512]{2,0,1:T(8,128)(2,1)S(1)} async-done(((bf16[16,32,512]{2,0,1:T(8,128)(2,1)}), bf16[16,32,512]{2,0,1:T(8,128)(2,1)S(1)}, u32[]{:S(2)}, u32[]{:S(2)}) %all-to-all-start.2) | async-done | bytes 524320 | tf_op jit(solution)/shard_map/all_to_all | solution.py:38
  108.3 1.1 fusion.29
  109.4 0.0 all-gather.2.cloned.1.call-done
  109.4 52.4 %fusion.8 = f32[4096,2048]{1,0:T(8,128)} fusion(bf16[1024,4096]{1,0:T(8,128)(2,1)} %all-gather.2.cloned.1.call-done, bf16[512,512]{1,0:T(8,128)(2,1)S(1)} %get-tuple-element.14, bf16[512,512]{1,0:T(8,128)(2,1)S(1)} %get-tuple-element.13, bf16[512,512]{1,0:T(8,128)(2,1)S(1)} %get-tuple-element.4, bf16[512,512]{1,0:T(8,128)(2,1)S(1)} %get-tuple-element.12, ...), kind=kOutput, calls=%fused_computation.14 | convolution fusion | flops 17213423616 | bytes 45088768 | tf_op jit(solution)/shard_map/dot_general | solution.py:14
  161.8 18.9 %fusion.6 = (bf16[1,4096,512]{2,1,0:T(8,128)(2,1)}, bf16[1,4096,512]{2,1,0:T(8,128)(2,1)}, bf16[1,4096,512]{2,1,0:T(8,128)(2,1)}, bf16[1,4096,512]{2,1,0:T(8,128)(2,1)}) fusion(f32[4096,2048]{1,0:T(8,128)} %fusion.8), kind=kLoop, calls=%fused_computation.12 | loop fusion | flops 16777216 | bytes 50331648 | tf_op jit(solution)/shard_map/stack | solution.py:68
  180.7 11.5 %pad_maximum_fusion = (bf16[2,4096,512]{2,1,0:T(8,128)(2,1)}, bf16[2,4096,512]{2,1,0:T(8,128)(2,1)}) fusion(bf16[1,4096,512]{2,1,0:T(8,128)(2,1)} %get-tuple-element.10, bf16[1,4096,512]{2,1,0:T(8,128)(2,1)} %get-tuple-element.11, bf16[1,4096,512]{2,1,0:T(8,128)(2,1)} %get-tuple-element.9, bf16[1,4096,512]{2,1,0:T(8,128)(2,1)} %get-tuple-element.8), kind=kLoop, calls=%fused_computation.8 | loop fusion | flops 8388608 | bytes 33554432 | tf_op jit(solution)/shard_map/stack | solution.py:68
  (3 shorter events, 0.0 us)
Async XLA Ops:
  8.7 16.3 %all-to-all-start = ((bf16[16,32,128]{2,0,1:T(8,128)(2,1)}), bf16[16,32,128]{2,0,1:T(8,128)(2,1)S(1)}, u32[]{:S(2)}, u32[]{:S(2)}) async-start(bf16[16,32,128]{2,0,1:T(8,128)(2,1)} %copy_bitcast_fusion.3), calls=%async_computation | async-start | bytes 262144 | tf_op jit(solution)/shard_map/all_to_all | solution.py:57
  17.3 92.1 %all-gather.2.cloned.1.call-start = ((), (), s32[]{:S(2)}) async-start(), calls=%async_computation.4 | async-start | bytes 8650752 | tf_op jit(solution)/shard_map/all_gather | solution.py:61
  50.6 39.2 %all-to-all-start.3 = ((bf16[16,32,512]{2,0,1:T(8,128)(2,1)}), bf16[16,32,512]{2,0,1:T(8,128)(2,1)S(1)}, u32[]{:S(2)}, u32[]{:S(2)}) async-start(bf16[16,32,512]{2,0,1:T(8,128)(2,1)} %bitcast.54), calls=%async_computation.3 | async-start | bytes 1048576 | tf_op jit(solution)/shard_map/all_to_all | solution.py:39
  89.8 18.5 %all-to-all-start.2 = ((bf16[16,32,512]{2,0,1:T(8,128)(2,1)}), bf16[16,32,512]{2,0,1:T(8,128)(2,1)S(1)}, u32[]{:S(2)}, u32[]{:S(2)}) async-start(bf16[16,32,512]{2,0,1:T(8,128)(2,1)} %bitcast.55), calls=%async_computation.2 | async-start | bytes 1048576 | tf_op jit(solution)/shard_map/all_to_all | solution.py:38
Sparse Core Ops, SparseCore 0:
  37.2 62.9 all-gather.1
where the time goes:
time: 200 us; the launch traced here: 199 us
  matrix products  52.4 us (26%)
  blocking collectives  51.7 us (26%)
  other arithmetic  34 us (17%)
  starting transfers between devices  20.9 us (10%)
  between operations  17.3 us (9%)
  waiting for transfers between devices  14.3 us (7%)
  local copies, waits for them, and re-layouts  8.55 us (4%)
    dot_general x1, matrix products, contract(): lax.dot_general(left_side, right_side, (((0,), (0,)), ((), ())), preferre...  52.4 us
    another operation x2, other arithmetic, on_device(): return (jnp.stack(real_out, axis=0), jnp.stack(imag_out, axis=0))  30.5 us
    unnamed x1, blocking collectives  15.7 us
    all_gather x1, blocking collectives, on_device(): lax.all_gather(matrix_imag, 'row', axis=1, tiled=True)  12.7 us
    all_gather x1, blocking collectives, on_device(): lax.all_gather(matrix_real, 'row', axis=1, tiled=True)  12 us
    all_to_all x1, blocking collectives, on_device(): lax.all_to_all(matrix_imag, 'col', split_axis=1, concat_axis=0, tiled=True)  11.3 us
    all_to_all x1, starting transfers between devices, on_device(): lax.all_to_all(matrix_real, 'col', split_axis=1, concat_axis=0, tiled=True)  8.59 us
    all_to_all x1, waiting for transfers between devices, on_device(): lax.all_to_all(spread_real, 'col', split_axis=1, concat_axis=0, tiled=True)  7.6 us
  transfers between devices with their start and end apart: 4, of which 2 were waited for; matrix products, arithmetic and copies ran while one was open for 5% of the time, Pallas kernels for 0%

commit v1 on v0

--- a/solution.py
+++ b/solution.py
@@ -31,7 +31,9 @@
     )
     gap = lookup(all_conduction, conduction_energy) - lookup(all_valence, valence_energy)
     spread_real, spread_imag = (
-        lax.all_gather(matrix_real, "row", axis=1, tiled=True),
+        jnp.concatenate(
+            lax.all_to_all(jnp.stack([matrix_real] * lax.axis_size("row")), "row", 0, 0), axis=1
+        ),
         lax.all_gather(matrix_imag, "row", axis=1, tiled=True),
     )
     column_real, column_imag = (

time: 200 us -> 198 us (0.990)
  blocking collectives: 51.7 us -> 40.2 us
  starting transfers between devices: 20.9 us -> 28.1 us
  local copies, waits for them, and re-layouts: 8.55 us -> 10.6 us
    all_gather x1 -> x0, blocking collectives: 12 us -> none  [on_device(): lax.all_gather(matrix_real, 'row', axis=1, tiled=True)]
    all_to_all x0 -> x1, starting transfers between devices: none -> 5.03 us  [on_device(): lax.all_to_all(jnp.stack([matrix_real] * lax.axis_size('row')), 'row', 0, 0)]
    all_to_all x1, starting transfers between devices: 5.45 us -> 8.11 us  [on_device(): lax.all_to_all(spread_imag, 'col', split_axis=1, concat_axis=0, tiled=True)]
  transfers between devices with their start and end apart: 4 -> 5, of which waited for: 2 -> 2; matrix products, arithmetic and copies ran while one was open for 5% -> 6% of each run, Pallas kernels for 0% -> 0%
where the time goes in v1:
time: 198 us
  matrix products  52.5 us (27%)
  blocking collectives  40.2 us (20%)
  other arithmetic  34 us (17%)
  starting transfers between devices  28.1 us (14%)
  between operations  17.4 us (9%)
  waiting for transfers between devices  14.9 us (8%)
  local copies, waits for them, and re-layouts  10.6 us (5%)
    dot_general x1, matrix products, contract(): lax.dot_general(left_side, right_side, (((0,), (0,)), ((), ())), preferre...  52.5 us
    another operation x2, other arithmetic, on_device(): return (jnp.stack(real_out, axis=0), jnp.stack(imag_out, axis=0))  30.5 us
    unnamed x1, blocking collectives  14.8 us
    all_gather x1, blocking collectives, on_device(): lax.all_gather(matrix_imag, 'row', axis=1, tiled=True)  14.2 us
    all_to_all x1, blocking collectives, on_device(): lax.all_to_all(matrix_imag, 'col', split_axis=1, concat_axis=0, tiled=True)  11.3 us
    all_to_all x1, starting transfers between devices, on_device(): lax.all_to_all(matrix_real, 'col', split_axis=1, concat_axis=0, tiled=True)  8.59 us
    all_to_all x1, waiting for transfers between devices, on_device(): lax.all_to_all(spread_real, 'col', split_axis=1, concat_axis=0, tiled=True)  8.15 us
    all_to_all x1, starting transfers between devices, on_device(): lax.all_to_all(spread_imag, 'col', split_axis=1, concat_axis=0, tiled=True)  8.11 us
  transfers between devices with their start and end apart: 5, of which 2 were waited for; matrix products, arithmetic and copies ran while one was open for 6% of the time, Pallas kernels for 0%

profile of v1, /device:TPU:1, one launch (start us, length us, event | category | flops | bytes accessed | tf_op | source)
XLA Modules:
  0.0 197.8 jit_solution(16521052743843318652)
XLA Ops:
  7.2 1.6 copy_bitcast_fusion.2
  8.8 8.6 %all-to-all-start = ((bf16[16,32,128]{2,0,1:T(8,128)(2,1)}), bf16[16,32,128]{2,0,1:T(8,128)(2,1)S(1)}, u32[]{:S(2)}, u32[]{:S(2)}) async-start(bf16[16,32,128]{2,0,1:T(8,128)(2,1)} %copy_bitcast_fusion.2), calls=%async_computation | async-start | bytes 262144 | tf_op jit(solution)/shard_map/all_to_all | solution.py:59
  17.4 0.0 all-gather.2.cloned.1.call-start
  17.4 0.9 copy_bitcast_fusion.1
  18.3 6.7 %all-to-all-done = bf16[16,32,128]{2,0,1:T(8,128)(2,1)S(1)} async-done(((bf16[16,32,128]{2,0,1:T(8,128)(2,1)}), bf16[16,32,128]{2,0,1:T(8,128)(2,1)S(1)}, u32[]{:S(2)}, u32[]{:S(2)}) %all-to-all-start) | async-done | bytes 131104 | tf_op jit(solution)/shard_map/all_to_all | solution.py:59
  25.1 11.3 %all_to_all.69 = bf16[16,32,128]{2,0,1:T(8,128)(2,1)S(1)} all-to-all(bf16[16,32,128]{2,0,1:T(8,128)(2,1)S(1)} %copy_bitcast_fusion.1), channel_id=1, replica_groups=mesh['row'=4,'col'=32] {'col'}, dimensions={1} | all-to-all | bytes 262144 | tf_op jit(solution)/shard_map/all_to_all | solution.py:60
  36.3 0.7 pad_maximum_fusion.2
  37.0 0.0 all-gather.2.cloned.1.call-update
  37.1 1.7 stack.25
  38.8 5.0 %all-to-all-start.2 = ((bf16[4,16,4096]{2,1,0:T(8,128)(2,1)}), bf16[4,16,4096]{2,1,0:T(8,128)(2,1)S(1)}, u32[]{:S(2)}, u32[]{:S(2)}) async-start(bf16[4,16,4096]{2,1,0:T(8,128)(2,1)} %stack.25), calls=%async_computation.2 | async-start | bytes 1048576 | tf_op jit(solution)/shard_map/all_to_all | solution.py:35
  43.8 14.2 %all_gather.15 = bf16[16,16384]{1,0:T(8,128)(2,1)S(1)} all-gather(bf16[16,4096]{1,0:T(8,128)(2,1)} %param.8), channel_id=1, replica_groups=mesh['row'=4,'col'=32] {'row'}, dimensions={1}, use_global_device_ids=true | all-gather | bytes 655360 | tf_op jit(solution)/shard_map/all_gather | solution.py:37
  58.0 0.9 copy.29
  58.8 0.0 all-to-all-done.2
  58.8 8.1 %all-to-all-start.4 = ((bf16[16,32,512]{2,0,1:T(8,128)(2,1)}), bf16[16,32,512]{2,0,1:T(8,128)(2,1)S(1)}, u32[]{:S(2)}, u32[]{:S(2)}) async-start(bf16[16,32,512]{2,0,1:T(8,128)(2,1)} %bitcast.52), calls=%async_computation.4 | async-start | bytes 1048576 | tf_op jit(solution)/shard_map/all_to_all | solution.py:41
  67.0 1.3 dynamic-slice
  68.9 0.9 dynamic-update-slice
  69.8 0.8 dynamic-update-slice.1
  70.6 14.8 %all-reduce.2 = (s32[512]{0:T(512)S(1)}, s32[512]{0:T(512)S(1)}) all-reduce(s32[512]{0:T(512)S(1)} %dynamic-update-slice, s32[512]{0:T(512)S(1)} %dynamic-update-slice.1), channel_id=1, replica_groups=mesh['row'=4,'col'=32] {'col'}, use_global_device_ids=true, to_apply=%add | all-reduce | flops 1024 | bytes 8192
  85.4 0.7 select_reduce_fusion.1
  86.1 0.7 select_reduce_fusion
  86.9 0.4 copy.20
  87.3 0.4 all_to_all.60
  87.7 1.1 copy.21
  88.7 0.0 all-to-all-done.4
  88.8 6.4 %all-to-all-start.3 = ((bf16[16,32,512]{2,0,1:T(8,128)(2,1)}), bf16[16,32,512]{2,0,1:T(8,128)(2,1)S(1)}, u32[]{:S(2)}, u32[]{:S(2)}) async-start(bf16[16,32,512]{2,0,1:T(8,128)(2,1)} %copy.21), calls=%async_computation.3 | async-start | bytes 1048576 | tf_op jit(solution)/shard_map/all_to_all | solution.py:40
  95.2 0.7 fusion.33
  98.5 0.2 fusion.24
  98.7 8.2 %all-to-all-done.3 = bf16[16,32,512]{2,0,1:T(8,128)(2,1)S(1)} async-done(((bf16[16,32,512]{2,0,1:T(8,128)(2,1)}), bf16[16,32,512]{2,0,1:T(8,128)(2,1)S(1)}, u32[]{:S(2)}, u32[]{:S(2)}) %all-to-all-start.3) | async-done | bytes 524320 | tf_op jit(solution)/shard_map/all_to_all | solution.py:40
  106.9 1.1 fusion.29
  108.0 52.5 %fusion.8 = f32[4096,2048]{1,0:T(8,128)} fusion(bf16[1024,4096]{1,0:T(8,128)(2,1)} %all-gather.2.cloned.1.call-done, bf16[512,512]{1,0:T(8,128)(2,1)S(1)} %get-tuple-element.14, bf16[512,512]{1,0:T(8,128)(2,1)S(1)} %get-tuple-element.13, bf16[512,512]{1,0:T(8,128)(2,1)S(1)} %get-tuple-element.4, bf16[512,512]{1,0:T(8,128)(2,1)S(1)} %get-tuple-element.12, ...), kind=kOutput, calls=%fused_computation.14 | convolution fusion | flops 17213423616 | bytes 45088768 | tf_op jit(solution)/shard_map/dot_general | solution.py:14
  160.4 18.9 %fusion.6 = (bf16[1,4096,512]{2,1,0:T(8,128)(2,1)}, bf16[1,4096,512]{2,1,0:T(8,128)(2,1)}, bf16[1,4096,512]{2,1,0:T(8,128)(2,1)}, bf16[1,4096,512]{2,1,0:T(8,128)(2,1)}) fusion(f32[4096,2048]{1,0:T(8,128)} %fusion.8), kind=kLoop, calls=%fused_computation.12 | loop fusion | flops 16777216 | bytes 50331648 | tf_op jit(solution)/shard_map/stack | solution.py:70
  179.4 11.5 %pad_maximum_fusion = (bf16[2,4096,512]{2,1,0:T(8,128)(2,1)}, bf16[2,4096,512]{2,1,0:T(8,128)(2,1)}) fusion(bf16[1,4096,512]{2,1,0:T(8,128)(2,1)} %get-tuple-element.10, bf16[1,4096,512]{2,1,0:T(8,128)(2,1)} %get-tuple-element.11, bf16[1,4096,512]{2,1,0:T(8,128)(2,1)} %get-tuple-element.9, bf16[1,4096,512]{2,1,0:T(8,128)(2,1)} %get-tuple-element.8), kind=kLoop, calls=%fused_computation.8 | loop fusion | flops 8388608 | bytes 33554432 | tf_op jit(solution)/shard_map/stack | solution.py:70
  (6 shorter events, 0.0 us)
Async XLA Ops:
  7.2 88.0 %copy-start = (f32[2]{0:T(128)S(1)}, f32[2]{0:T(128)}, u32[]{:S(2)}) copy-start(f32[2]{0:T(128)} %param.13) | copy-start | bytes 28
  8.8 16.3 %all-to-all-start = ((bf16[16,32,128]{2,0,1:T(8,128)(2,1)}), bf16[16,32,128]{2,0,1:T(8,128)(2,1)S(1)}, u32[]{:S(2)}, u32[]{:S(2)}) async-start(bf16[16,32,128]{2,0,1:T(8,128)(2,1)} %copy_bitcast_fusion.2), calls=%async_computation | async-start | bytes 262144 | tf_op jit(solution)/shard_map/all_to_all | solution.py:59
  17.4 90.6 %all-gather.2.cloned.1.call-start = ((), (), s32[]{:S(2)}) async-start(), calls=%async_computation.5 | async-start | bytes 8650752 | tf_op jit(solution)/shard_map/all_gather | solution.py:63
  38.8 20.0 %all-to-all-start.2 = ((bf16[4,16,4096]{2,1,0:T(8,128)(2,1)}), bf16[4,16,4096]{2,1,0:T(8,128)(2,1)S(1)}, u32[]{:S(2)}, u32[]{:S(2)}) async-start(bf16[4,16,4096]{2,1,0:T(8,128)(2,1)} %stack.25), calls=%async_computation.2 | async-start | bytes 1048576 | tf_op jit(solution)/shard_map/all_to_all | solution.py:35
  58.8 29.9 %all-to-all-start.4 = ((bf16[16,32,512]{2,0,1:T(8,128)(2,1)}), bf16[16,32,512]{2,0,1:T(8,128)(2,1)S(1)}, u32[]{:S(2)}, u32[]{:S(2)}) async-start(bf16[16,32,512]{2,0,1:T(8,128)(2,1)} %bitcast.52), calls=%async_computation.4 | async-start | bytes 1048576 | tf_op jit(solution)/shard_map/all_to_all | solution.py:41
  88.8 18.1 %all-to-all-start.3 = ((bf16[16,32,512]{2,0,1:T(8,128)(2,1)}), bf16[16,32,512]{2,0,1:T(8,128)(2,1)S(1)}, u32[]{:S(2)}, u32[]{:S(2)}) async-start(bf16[16,32,512]{2,0,1:T(8,128)(2,1)} %copy.21), calls=%async_computation.3 | async-start | bytes 1048576 | tf_op jit(solution)/shard_map/all_to_all | solution.py:40
Sparse Core Ops, SparseCore 0:
  37.2 64.1 all-gather.1
